TPU v7x, 32 devices: a whole 2x2x4 slice. The times are simulated.
32 devices in a mesh: groups: 2 (over y), gx: 4 (over z), gy: 4 (over x, core).
Axes of the slice: x: 2, y: 2, z: 4, core: 2. Of those that a mesh axis runs over, the one named last changes fastest.
Arguments:
- tokens: bfloat16 [40, 8192], P(('groups', 'gx'), 'gy'), parts along dimension 0, may hold values from -180 to 180, as said below
- norm_gain: float32 [8192], P('gy'), may hold values from 0.1 to 1.9
- w_gate: bfloat16 [8192, 24576], P('gy', 'gx'), may hold values from -0.0625 to 0.0625
- w_up: bfloat16 [8192, 24576], P('gy', 'gx'), may hold values from -0.0625 to 0.0625
- w_down: bfloat16 [24576, 8192], P('gx', 'gy'), may hold values from -0.0390625 to 0.0390625
Outputs:
- mixed: bfloat16 [40, 8192], P(('groups', 'gx'), 'gy'), parts along dimension 0
There are 2 independent parts, one for each index of `groups`. A program takes and returns all parts, laid end to end along the dimension named above; an argument that names none is the same for every part. Nothing has to cross between parts.
Inputs may be any that keep to these rules, and one draw needn't show every extreme that they name: tokens are real-valued activations of order one to some tens.
All inputs are finite; a program needn't handle non-finite values.
Results may differ from a plain program's by a relative error of at most 0.0064.
Values may be sent and summed in bfloat16 or wider, within the bound.
No kernel may reach another device: no remote copies, remote signals or barrier semaphores. Data moves between devices by JAX's collectives and lax.ppermute only.
A program may use at most 192 MiB of HBM per device.

v0:
```python
import jax
import jax.numpy as jnp
from jax import lax
from jax.sharding import PartitionSpec as P

D = 8192
epsilon = 1e-06


def activate(both, width):
    gate = both[:, :width]
    up_part = both[:, width:]
    return (jax.nn.silu(gate) * up_part).astype(jnp.bfloat16)


def local(tokens, norm_gain, w_gate, w_up, w_down):
    values = tokens.astype(jnp.float32)
    local_sq = jnp.sum(values * values, axis=1)
    total_sq = lax.psum(local_sq, "gy")
    inverse = lax.rsqrt(total_sq / D + epsilon)
    normed = (values * inverse[:, None] * norm_gain[None, :]).astype(jnp.bfloat16)
    width = w_gate.shape[1]
    piece = lax.all_gather(normed, "gx", axis=0, tiled=True)
    gate_part = jnp.dot(piece, w_gate, preferred_element_type=jnp.float32)
    up_part = jnp.dot(piece, w_up, preferred_element_type=jnp.float32)
    partial_value = jnp.concatenate([gate_part, up_part], axis=1)
    summed = lax.psum(partial_value, "gy")
    hidden = activate(summed, width)
    result = lax.psum_scatter(
        jnp.dot(hidden, w_down, preferred_element_type=jnp.float32),
        "gx",
        scatter_dimension=0,
        tiled=True,
    )
    return result.astype(jnp.bfloat16)


def solution(mesh):
    in_specs = (P(("groups", "gx"), "gy"), P("gy"), P("gy", "gx"), P("gy", "gx"), P("gx", "gy"))
    out_specs = P(("groups", "gx"), "gy")
    return jax.shard_map(local, mesh=mesh, in_specs=in_specs, out_specs=out_specs, check_vma=False)
```

profile of v0, /device:TPU:0, one launch (start us, length us, event | category | flops | bytes accessed | tf_op | source)
XLA Modules:
  0.0 128.5 jit_solution(15527987693795817400)
XLA Ops:
  6.5 0.0 all-reduce.4.cloned.1.call-start
  6.5 0.9 fusion.5
  7.4 8.3 %psum.14 = f32[5]{0:T(128)S(1)} all-reduce(f32[5]{0:T(128)S(1)} %fusion.5), channel_id=1, replica_groups=mesh['groups'=2,'gx'=4,'gy'=4] {'gy'}, use_global_device_ids=true, to_apply=%region_1.0 | all-reduce | flops 5 | bytes 40 | tf_op jit(solution)/shard_map/psum | solution.py:19
  15.8 0.8 fusion.8
  16.6 13.6 %all-gather = bf16[4,5,2048]{2,1,0:T(8,128)(2,1)S(1)} all-gather(bf16[1,5,2048]{2,1,0:T(8,128)(2,1)S(1)} %fusion.8), channel_id=1, replica_groups=mesh['groups'=2,'gx'=4,'gy'=4] {'gx'}, dimensions={0}, use_global_device_ids=true | all-gather | bytes 102400 | tf_op jit(solution)/shard_map/all_gather | solution.py:23
  30.3 9.9 %fusion.10 = f32[20,6144]{1,0:T(8,128)S(1)} fusion(bf16[20,2048]{1,0:T(8,128)(2,1)S(1)} %reshape.3, bf16[2048,6144]{1,0:T(8,128)(2,1)} %param.7), kind=kOutput, calls=%fused_computation.14 | convolution fusion | flops 503316480 | bytes 25739264 | tf_op jit(solution)/shard_map/dot_general | solution.py:24
  40.2 9.9 %fusion.11 = f32[20,6144]{1,0:T(8,128)S(1)} fusion(bf16[20,2048]{1,0:T(8,128)(2,1)S(1)} %reshape.3, bf16[2048,6144]{1,0:T(8,128)(2,1)} %param.8), kind=kOutput, calls=%fused_computation.15 | convolution fusion | flops 503316480 | bytes 25739264 | tf_op jit(solution)/shard_map/dot_general | solution.py:25
  50.1 0.0 copy-start
  50.1 1.1 pad_maximum_fusion
  51.2 0.0 all-reduce.4.cloned.1.call-update
  51.2 37.8 %all-reduce.4.cloned.1.call-done = f32[20,12288]{1,0:T(8,128)} async-done(((f32[20,12288]{1,0:T(8,128)}), f32[20,12288]{1,0:T(8,128)}) %all-reduce.4.cloned.1.call-update) | async-done | bytes 983056 | tf_op jit(solution)/shard_map/psum | solution.py:27
  89.0 10.2 %fusion.2 = f32[20,2048]{1,0:T(8,128)S(1)} fusion(bf16[6144,2048]{1,0:T(8,128)(2,1)} %param.9, f32[20,12288]{1,0:T(8,128)} %all-reduce.4.cloned.1.call-done), kind=kOutput, calls=%fused_computation.3 | convolution fusion | flops 504053760 | bytes 26312704 | tf_op jit(solution)/shard_map/dot_general | solution.py:30
  99.3 14.6 %fusion = f32[8,2048]{1,0:T(8,128)S(1)} fusion(f32[20,2048]{1,0:T(8,128)S(1)} %fusion.2), kind=kCustom, calls=%all-reduce-scatter | all-reduce-scatter fusion | flops 65537 | bytes 229888
  113.9 2.2 %collective-permute-start = (bf16[8,2048]{1,0:T(8,128)(2,1)S(1)}, bf16[8,2048]{1,0:T(8,128)(2,1)S(1)}, u32[]{:S(2)}, u32[]{:S(2)}) collective-permute-start(bf16[8,2048]{1,0:T(8,128)(2,1)S(1)} %convert), channel_id=1, source_target_pairs={{0,4},{4,8},{8,12},{1,5},{5,9},{9,13},{2,6},{6,10},{10,14},{3,7},{... | collective-permute-start | bytes 98312
  116.2 3.2 %collective-permute-start.1 = (bf16[1,2048]{1,0:T(2,128)(2,1)S(1)}, bf16[1,2048]{1,0:T(2,128)(2,1)S(1)}, u32[]{:S(2)}, u32[]{:S(2)}) collective-permute-start(bf16[1,2048]{1,0:T(2,128)(2,1)S(1)} %slice.10), channel_id=1, source_target_pairs={{0,8},{4,12},{1,9},{5,13},{2,10},{6,14},{3,11},{7,15},{16,24},{20,... | collective-permute-start | bytes 12296
  119.4 0.0 copy-done
  119.4 0.6 dynamic-slice.4
  120.6 0.1 collective-permute-done.1
  120.7 0.0 collective-permute-done
  120.7 0.3 concatenate.4
  121.0 0.6 dynamic-slice_convert_fusion
  (4 shorter events, 0.1 us)
Async XLA Ops:
  6.5 82.5 %all-reduce.4.cloned.1.call-start = ((), (), s32[]{:S(2)}) async-start(), calls=%async_computation | async-start | bytes 2359296 | tf_op jit(solution)/shard_map/psum | solution.py:27
  50.1 69.3 %copy-start = (u32[32]{0:T(128)S(1)}, u32[32]{0:T(128)}, u32[]{:S(2)}) copy-start(u32[32]{0:T(128)} %constant.13) | copy-start | bytes 388
  113.9 6.8 %collective-permute-start = (bf16[8,2048]{1,0:T(8,128)(2,1)S(1)}, bf16[8,2048]{1,0:T(8,128)(2,1)S(1)}, u32[]{:S(2)}, u32[]{:S(2)}) collective-permute-start(bf16[8,2048]{1,0:T(8,128)(2,1)S(1)} %convert), channel_id=1, source_target_pairs={{0,4},{4,8},{8,12},{1,5},{5,9},{9,13},{2,6},{6,10},{10,14},{3,7},{... | collective-permute-start | bytes 98312
  116.2 4.5 %collective-permute-start.1 = (bf16[1,2048]{1,0:T(2,128)(2,1)S(1)}, bf16[1,2048]{1,0:T(2,128)(2,1)S(1)}, u32[]{:S(2)}, u32[]{:S(2)}) collective-permute-start(bf16[1,2048]{1,0:T(2,128)(2,1)S(1)} %slice.10), channel_id=1, source_target_pairs={{0,8},{4,12},{1,9},{5,13},{2,10},{6,14},{3,11},{7,15},{16,24},{20,... | collective-permute-start | bytes 12296
Sparse Core Ops, SparseCore 0:
  51.4 37.6 all-reduce.3
where the time goes:
time: 129 us
  waiting for transfers between devices  37.9 us (29%)
  blocking collectives  36.6 us (28%)
  matrix products  30 us (23%)
  between operations  14.1 us (11%)
  starting transfers between devices  5.42 us (4%)
  other arithmetic  2.87 us (2%)
  local copies, waits for them, and re-layouts  1.57 us (1%)
    psum x1, waiting for transfers between devices, local(): summed = lax.psum(partial_value, 'gy')  37.8 us
    unnamed x1, blocking collectives  14.6 us
    all_gather x1, blocking collectives, local(): piece = lax.all_gather(normed, 'gx', axis=0, tiled=True)  13.6 us
    dot_general x1, matrix products, local(): jnp.dot(hidden, w_down, preferred_element_type=jnp.float32)  10.2 us
    dot_general x1, matrix products, local(): up_part = jnp.dot(piece, w_up, preferred_element_type=jnp.float32)  9.91 us
    dot_general x1, matrix products, local(): gate_part = jnp.dot(piece, w_gate, preferred_element_type=jnp.float32)  9.91 us
    psum x1, blocking collectives, local(): total_sq = lax.psum(local_sq, 'gy')  8.34 us
    unnamed x2, starting transfers between devices  5.41 us
  transfers between devices with their start and end apart: 3, of which 2 were waited for; matrix products, arithmetic and copies ran while one was open for 0% of the time, Pallas kernels for 0%

commit v1 on v0

--- a/solution.py
+++ b/solution.py
@@ -20,7 +20,16 @@
     inverse = lax.rsqrt(total_sq / D + epsilon)
     normed = (values * inverse[:, None] * norm_gain[None, :]).astype(jnp.bfloat16)
     width = w_gate.shape[1]
-    piece = lax.all_gather(normed, "gx", axis=0, tiled=True)
+    ways = lax.axis_size("gx")
+    up = [(d, (d + 1) % ways) for d in range(ways)]
+    down = [(d, (d - 1) % ways) for d in range(ways)]
+    earlier, later = ([normed], [normed])
+    for _ in range(ways // 2):
+        earlier.append(lax.ppermute(earlier[-1], "gx", up))
+    for _ in range((ways - 1) // 2):
+        later.append(lax.ppermute(later[-1], "gx", down))
+    line = jnp.concatenate([*earlier[::-1], *later[1:]], axis=0)
+    piece = jnp.roll(line, (lax.axis_index("gx") - ways // 2) * normed.shape[0], axis=0)
     gate_part = jnp.dot(piece, w_gate, preferred_element_type=jnp.float32)
     up_part = jnp.dot(piece, w_up, preferred_element_type=jnp.float32)
     partial_value = jnp.concatenate([gate_part, up_part], axis=1)

time: 129 us -> 124 us (0.961)
  blocking collectives: 36.6 us -> 23 us
  waiting for transfers between devices: 37.9 us -> 42.6 us
  starting transfers between devices: 5.42 us -> 9.29 us
    all_gather x1 -> x0, blocking collectives: 13.6 us -> none  [local(): piece = lax.all_gather(normed, 'gx', axis=0, tiled=True)]
    ppermute x0 -> x3, waiting for transfers between devices: none -> 7.7 us  [the longest x2 7.69 us: local(): earlier.append(lax.ppermute(earlier[-1], 'gx', up))]
    ppermute x0 -> x3, starting transfers between devices: none -> 3.87 us  [the longest x1 2.25 us: local(): later.append(lax.ppermute(later[-1], 'gx', down))]
    psum x1, waiting for transfers between devices: 37.8 us -> 34.7 us  [local(): summed = lax.psum(partial_value, 'gy')]
  transfers between devices with their start and end apart: 3 -> 6, of which waited for: 2 -> 4; matrix products, arithmetic and copies ran while one was open for 0% -> 0% of each run, Pallas kernels for 0% -> 0%
where the time goes in v1:
time: 124 us
  waiting for transfers between devices  42.6 us (34%)
  matrix products  30 us (24%)
  blocking collectives  23 us (19%)
  between operations  14.1 us (11%)
  starting transfers between devices  9.29 us (7%)
  other arithmetic  2.88 us (2%)
  local copies, waits for them, and re-layouts  2.14 us (2%)
    psum x1, waiting for transfers between devices, local(): summed = lax.psum(partial_value, 'gy')  34.7 us
    unnamed x1, blocking collectives  14.6 us
    dot_general x1, matrix products, local(): jnp.dot(hidden, w_down, preferred_element_type=jnp.float32)  10.2 us
    dot_general x1, matrix products, local(): gate_part = jnp.dot(piece, w_gate, preferred_element_type=jnp.float32)  9.91 us
    dot_general x1, matrix products, local(): up_part = jnp.dot(piece, w_up, preferred_element_type=jnp.float32)  9.9 us
    psum x1, blocking collectives, local(): total_sq = lax.psum(local_sq, 'gy')  8.34 us
    ppermute x2, waiting for transfers between devices, local(): earlier.append(lax.ppermute(earlier[-1], 'gx', up))  7.69 us
    unnamed x2, starting transfers between devices  5.41 us
  transfers between devices with their start and end apart: 6, of which 4 were waited for; matrix products, arithmetic and copies ran while one was open for 0% of the time, Pallas kernels for 0%

profile of v1, /device:TPU:0, one launch (start us, length us, event | category | flops | bytes accessed | tf_op | source)
XLA Modules:
  0.0 124.0 jit_solution(17886467316569628078)
XLA Ops:
  6.5 0.0 all-reduce.4.cloned.1.call-start
  6.5 0.9 fusion.9
  7.4 8.3 %psum.14 = f32[5]{0:T(128)S(1)} all-reduce(f32[5]{0:T(128)S(1)} %fusion.9), channel_id=1, replica_groups=mesh['groups'=2,'gx'=4,'gy'=4] {'gy'}, use_global_device_ids=true, to_apply=%region_1.0 | all-reduce | flops 5 | bytes 40 | tf_op jit(solution)/shard_map/psum | solution.py:19
  15.8 0.8 fusion.11
  16.6 1.6 %collective-permute-start = (bf16[5,2048]{1,0:T(8,128)(2,1)S(1)}, bf16[5,2048]{1,0:T(8,128)(2,1)S(1)}, u32[]{:S(2)}, u32[]{:S(2)}) collective-permute-start(bf16[5,2048]{1,0:T(8,128)(2,1)S(1)} %fusion.11), channel_id=1, source_target_pairs={{0,4},{4,8},{8,12},{12,0},{1,5},{5,9},{9,13},{13,1},{2,6},{6,10},{... | collective-permute-start | bytes 61448 | tf_op jit(solution)/shard_map/ppermute | solution.py:28
  18.2 2.2 %collective-permute-start.2 = (bf16[5,2048]{1,0:T(8,128)(2,1)S(1)}, bf16[5,2048]{1,0:T(8,128)(2,1)S(1)}, u32[]{:S(2)}, u32[]{:S(2)}) collective-permute-start(bf16[5,2048]{1,0:T(8,128)(2,1)S(1)} %fusion.11), channel_id=1, source_target_pairs={{0,12},{4,0},{8,4},{12,8},{1,13},{5,1},{9,5},{13,9},{2,14},{6,2},{... | collective-permute-start | bytes 61448 | tf_op jit(solution)/shard_map/ppermute | solution.py:30
  20.5 2.0 %collective-permute-done = bf16[5,2048]{1,0:T(8,128)(2,1)S(1)} collective-permute-done((bf16[5,2048]{1,0:T(8,128)(2,1)S(1)}, bf16[5,2048]{1,0:T(8,128)(2,1)S(1)}, u32[]{:S(2)}, u32[]{:S(2)}) %collective-permute-start) | collective-permute-done | bytes 20512 | tf_op jit(solution)/shard_map/ppermute | solution.py:28
  22.5 0.0 collective-permute-start.1
  22.5 0.0 collective-permute-done.2
  22.5 5.7 %collective-permute-done.1 = bf16[5,2048]{1,0:T(8,128)(2,1)S(1)} collective-permute-done((bf16[5,2048]{1,0:T(8,128)(2,1)S(1)}, bf16[5,2048]{1,0:T(8,128)(2,1)S(1)}, u32[]{:S(2)}, u32[]{:S(2)}) %collective-permute-start.1) | collective-permute-done | bytes 20512 | tf_op jit(solution)/shard_map/ppermute | solution.py:28
  28.2 0.6 concatenate.9
  28.8 9.9 %fusion.7 = f32[20,6144]{1,0:T(8,128)S(1)} fusion(bf16[2048,6144]{1,0:T(8,128)(2,1)} %param.7, bf16[40,2048]{1,0:T(8,128)(2,1)S(1)} %concatenate.9, s32[]{:T(128)S(6)} %select_n.14), kind=kOutput, calls=%fused_computation.7 | convolution fusion | flops 503316480 | bytes 25755652 | tf_op jit(solution)/shard_map/dot_general | solution.py:33
  38.7 9.9 %fusion.5 = f32[20,6144]{1,0:T(8,128)S(1)} fusion(bf16[2048,6144]{1,0:T(8,128)(2,1)} %param.8, bf16[40,2048]{1,0:T(8,128)(2,1)S(1)} %concatenate.9, s32[]{:T(128)S(6)} %select_n.14), kind=kOutput, calls=%fused_computation.5 | convolution fusion | flops 503316480 | bytes 25755652 | tf_op jit(solution)/shard_map/dot_general | solution.py:34
  48.6 0.0 copy-start
  48.6 1.1 pad_maximum_fusion
  49.8 0.0 all-reduce.4.cloned.1.call-update
  49.8 34.7 %all-reduce.4.cloned.1.call-done = f32[20,12288]{1,0:T(8,128)} async-done(((f32[20,12288]{1,0:T(8,128)}), f32[20,12288]{1,0:T(8,128)}) %all-reduce.4.cloned.1.call-update) | async-done | bytes 983056 | tf_op jit(solution)/shard_map/psum | solution.py:36
  84.5 10.2 %fusion.2 = f32[20,2048]{1,0:T(8,128)S(1)} fusion(bf16[6144,2048]{1,0:T(8,128)(2,1)} %param.9, f32[20,12288]{1,0:T(8,128)} %all-reduce.4.cloned.1.call-done), kind=kOutput, calls=%fused_computation.3 | convolution fusion | flops 504053760 | bytes 26312704 | tf_op jit(solution)/shard_map/dot_general | solution.py:39
  94.7 14.6 %fusion = f32[8,2048]{1,0:T(8,128)S(1)} fusion(f32[20,2048]{1,0:T(8,128)S(1)} %fusion.2), kind=kCustom, calls=%all-reduce-scatter | all-reduce-scatter fusion | flops 65537 | bytes 229888
  109.4 2.2 %collective-permute-start.3 = (bf16[8,2048]{1,0:T(8,128)(2,1)S(1)}, bf16[8,2048]{1,0:T(8,128)(2,1)S(1)}, u32[]{:S(2)}, u32[]{:S(2)}) collective-permute-start(bf16[8,2048]{1,0:T(8,128)(2,1)S(1)} %convert), channel_id=1, source_target_pairs={{0,4},{4,8},{8,12},{1,5},{5,9},{9,13},{2,6},{6,10},{10,14},{3,7},{... | collective-permute-start | bytes 98312
  111.7 3.2 %collective-permute-start.4 = (bf16[1,2048]{1,0:T(2,128)(2,1)S(1)}, bf16[1,2048]{1,0:T(2,128)(2,1)S(1)}, u32[]{:S(2)}, u32[]{:S(2)}) collective-permute-start(bf16[1,2048]{1,0:T(2,128)(2,1)S(1)} %slice.10), channel_id=1, source_target_pairs={{0,8},{4,12},{1,9},{5,13},{2,10},{6,14},{3,11},{7,15},{16,24},{20,... | collective-permute-start | bytes 12296
  114.9 0.0 copy-done
  114.9 0.6 dynamic-slice.4
  116.1 0.1 collective-permute-done.4
  116.2 0.0 collective-permute-done.3
  116.2 0.3 concatenate.11
  116.5 0.6 dynamic-slice_convert_fusion
  (3 shorter events, 0.0 us)
Async XLA Ops:
  6.5 78.0 %all-reduce.4.cloned.1.call-start = ((), (), s32[]{:S(2)}) async-start(), calls=%async_computation | async-start | bytes 2359296 | tf_op jit(solution)/shard_map/psum | solution.py:36
  16.6 5.9 %collective-permute-start = (bf16[5,2048]{1,0:T(8,128)(2,1)S(1)}, bf16[5,2048]{1,0:T(8,128)(2,1)S(1)}, u32[]{:S(2)}, u32[]{:S(2)}) collective-permute-start(bf16[5,2048]{1,0:T(8,128)(2,1)S(1)} %fusion.11), channel_id=1, source_target_pairs={{0,4},{4,8},{8,12},{12,0},{1,5},{5,9},{9,13},{13,1},{2,6},{6,10},{... | collective-permute-start | bytes 61448 | tf_op jit(solution)/shard_map/ppermute | solution.py:28
  18.2 4.3 %collective-permute-start.2 = (bf16[5,2048]{1,0:T(8,128)(2,1)S(1)}, bf16[5,2048]{1,0:T(8,128)(2,1)S(1)}, u32[]{:S(2)}, u32[]{:S(2)}) collective-permute-start(bf16[5,2048]{1,0:T(8,128)(2,1)S(1)} %fusion.11), channel_id=1, source_target_pairs={{0,12},{4,0},{8,4},{12,8},{1,13},{5,1},{9,5},{13,9},{2,14},{6,2},{... | collective-permute-start | bytes 61448 | tf_op jit(solution)/shard_map/ppermute | solution.py:30
  22.5 5.7 %collective-permute-start.1 = (bf16[5,2048]{1,0:T(8,128)(2,1)S(1)}, bf16[5,2048]{1,0:T(8,128)(2,1)S(1)}, u32[]{:S(2)}, u32[]{:S(2)}) collective-permute-start(bf16[5,2048]{1,0:T(8,128)(2,1)S(1)} %collective-permute-done), channel_id=1, source_target_pairs={{0,4},{4,8},{8,12},{12,0},{1,5},{5,9},{9,13},{13,1},{2,6},{6,10},{... | collective-permute-start | bytes 61448 | tf_op jit(solution)/shard_map/ppermute | solution.py:28
  48.6 66.2 %copy-start = (u32[32]{0:T(128)S(1)}, u32[32]{0:T(128)}, u32[]{:S(2)}) copy-start(u32[32]{0:T(128)} %constant.42) | copy-start | bytes 388
  109.4 6.8 %collective-permute-start.3 = (bf16[8,2048]{1,0:T(8,128)(2,1)S(1)}, bf16[8,2048]{1,0:T(8,128)(2,1)S(1)}, u32[]{:S(2)}, u32[]{:S(2)}) collective-permute-start(bf16[8,2048]{1,0:T(8,128)(2,1)S(1)} %convert), channel_id=1, source_target_pairs={{0,4},{4,8},{8,12},{1,5},{5,9},{9,13},{2,6},{6,10},{10,14},{3,7},{... | collective-permute-start | bytes 98312
  111.7 4.5 %collective-permute-start.4 = (bf16[1,2048]{1,0:T(2,128)(2,1)S(1)}, bf16[1,2048]{1,0:T(2,128)(2,1)S(1)}, u32[]{:S(2)}, u32[]{:S(2)}) collective-permute-start(bf16[1,2048]{1,0:T(2,128)(2,1)S(1)} %slice.10), channel_id=1, source_target_pairs={{0,8},{4,12},{1,9},{5,13},{2,10},{6,14},{3,11},{7,15},{16,24},{20,... | collective-permute-start | bytes 12296
Sparse Core Ops, SparseCore 0:
  49.9 34.5 all-reduce.3
